TPU v7x, 32 devices: a whole 2x2x4 slice. The times are simulated.
32 devices in a mesh: tile: 8 (over z, x), chan: 4 (over y, core).
Axes of the slice: x: 2, y: 2, z: 4, core: 2. Of those that a mesh axis runs over, the one named last changes fastest.
Arguments:
- visibilities: float32 [4, 2048, 128], P('chan', 'tile'), may hold values from -6 to 6
- kernels: bfloat16 [4, 32, 2, 64, 128], P('chan'), may hold values from -0.75 to 0.75
- destination: int32 [4, 2048, 1], P('chan', 'tile'), may hold values from 0 to 7; in each aligned block of 256 rows (0 to 255, 256 to 511, ..., all dimensions but the last counted through in order) at most 96 rows name the same one
- cell: int32 [4, 2048], P('chan', 'tile'), may hold values from 0 to 2047
- plane: int32 [4, 2048], P('chan', 'tile'), may hold values from 0 to 31
Outputs:
- image: float32 [1024, 1024], P('chan', 'tile')
Inputs may be any that keep to these rules, and one draw needn't show every extreme that they name: `destination`: in the rows of one device (aligned blocks of 256 rows), no tile is named more than 96 times; some tile is named exactly 96 times in some devices' rows.
All inputs are finite; a program needn't handle non-finite values.
Results may differ from a plain program's by a relative error of at most 0.0059.
Values may be sent and summed in bfloat16 or wider, within the bound.
No kernel may reach another device: no remote copies, remote signals or barrier semaphores. Data moves between devices by JAX's collectives and lax.ppermute only.
A program may use at most 384 MiB of HBM per device.

v0:
```python
import math

import jax
import jax.numpy as jnp
from jax import lax
from jax.sharding import PartitionSpec as P
from jax.experimental import pallas as pl
from jax.experimental.pallas import tpu as pltpu

G = 8192
S = 64
NW = 32
P_SIZE = 1024
NF = 8


def block_patches(samples, kernel_rows):
    sample_count = samples.shape[1] // 2
    support = kernel_rows.shape[3] // 2
    vis_real = samples[:, :sample_count, None]
    vis_imag = samples[:, sample_count:, None]
    kern_real = kernel_rows[:, 0].astype(jnp.float32)
    kern_imag = kernel_rows[:, 1].astype(jnp.float32)
    full_real = (vis_real * kern_real - vis_imag * kern_imag).astype(jnp.bfloat16)
    full_imag = (vis_real * kern_imag + vis_imag * kern_real).astype(jnp.bfloat16)
    weighted_real = full_real[:, :, support:]
    weighted_imag = full_imag[:, :, support:]
    v_weighted = jnp.stack(
        [
            jnp.concatenate([weighted_real, weighted_imag], axis=-1),
            jnp.concatenate([-weighted_imag, weighted_real], axis=-1),
        ],
        1,
    )
    patch = jnp.einsum("bpkx,bpkn->bxn", kernel_rows, v_weighted, preferred_element_type=jnp.float32)
    return patch[:, :support, :]


PATCH_CHUNK = 128


def patch_kernel(plane_ref, samples_ref, u_ref, v_ref, out_ref):
    base = pl.program_id(0) * PATCH_CHUNK
    for j in range(PATCH_CHUNK):
        w = plane_ref[base + j]
        column = samples_ref[:, j : j + 1]
        vis_real = column[:S]
        vis_imag = column[S:]
        first = v_ref[w, 0].astype(jnp.float32)
        second = v_ref[w, 1].astype(jnp.float32)
        top = (vis_real * first + vis_imag * second).astype(jnp.bfloat16)
        bottom = (vis_real * second - vis_imag * first).astype(jnp.bfloat16)
        rhs = jnp.concatenate(
            [jnp.concatenate([top, bottom], axis=1), jnp.concatenate([bottom, -top], axis=1)], axis=0
        )
        both = jnp.dot(u_ref[w], rhs, preferred_element_type=jnp.float32)
        out_ref[j, 0] = both[:, : 2 * S].astype(jnp.bfloat16)
        out_ref[j, 1] = both[:, 2 * S :].astype(jnp.bfloat16)


def patches_rotated(samples, planes, kernel_set):
    slots = samples.shape[0]
    u_kernel = jnp.transpose(kernel_set[:, :, :, :S], (0, 3, 1, 2)).reshape(NW, S, 2 * S)
    v_real = kernel_set[:, 0, :, S:]
    v_imag = kernel_set[:, 1, :, S:]
    v_parts = jnp.stack(
        [jnp.concatenate([v_real, v_imag], axis=-1), jnp.concatenate([-v_imag, v_real], axis=-1)], axis=1
    )
    grid_spec = pltpu.PrefetchScalarGridSpec(
        num_scalar_prefetch=1,
        grid=(slots // PATCH_CHUNK,),
        in_specs=[
            pl.BlockSpec((2 * S, PATCH_CHUNK), lambda i, p: (0, i)),
            pl.BlockSpec((NW, S, 2 * S), lambda i, p: (0, 0, 0)),
            pl.BlockSpec((NW, 2, S, 2 * S), lambda i, p: (0, 0, 0, 0)),
        ],
        out_specs=pl.BlockSpec((PATCH_CHUNK, 2, S, 2 * S), lambda i, p: (i, 0, 0, 0)),
    )
    return pl.pallas_call(
        patch_kernel,
        grid_spec=grid_spec,
        out_shape=jax.ShapeDtypeStruct((slots, 2, S, 2 * S), jnp.bfloat16),
        cost_estimate=pl.CostEstimate(
            flops=2 * slots * S * 2 * S * 4 * S, transcendentals=0, bytes_accessed=slots * 2 * S * 2 * S * 2 * 2
        ),
    )(planes, jnp.transpose(samples), u_kernel, v_parts)


def phase_index(rows, cols):
    spacing = G // P_SIZE - 1
    return jnp.mod(rows[:, None] * (spacing * cols[None, :]), G)


def cos_sin_f32(index):
    angle = index.astype(jnp.float32) * (2.0 * math.pi / G)
    return jnp.cos(angle), jnp.sin(angle)


def local(visibilities, kernels, destination, cell, plane):
    tile_count = lax.axis_size("tile")
    tile_index = lax.axis_index("tile")
    samples = visibilities[0]
    kernel_set = kernels[0]
    owners = destination[0, :, 0]
    blocks = samples.shape[0]
    capacity = 3 * blocks // tile_count
    spacing = G // P_SIZE - 1

    tiles = jnp.arange(tile_count, dtype=jnp.int32)
    onehot = (owners[:, None] == tiles[None, :]).astype(jnp.int32)
    rank = jnp.sum(jnp.cumsum(onehot, axis=0) * onehot, axis=1) - 1
    slot = jnp.arange(capacity, dtype=jnp.int32)
    pick = (owners[None, None, :] == tiles[:, None, None]) & (rank[None, None, :] == slot[None, :, None])
    pick = pick.astype(jnp.float32).reshape(tile_count * capacity, blocks)
    packed_meta = (cell[0] * NW + plane[0]).astype(jnp.float32)
    routed = jnp.dot(
        pick, jnp.concatenate([samples, packed_meta[:, None]], axis=1), precision=lax.Precision.HIGHEST
    )
    send_samples = routed[:, : samples.shape[1]].reshape(tile_count, capacity, samples.shape[1])
    send_meta = routed[:, samples.shape[1]].reshape(tile_count, capacity)
    meta_row = jnp.pad(send_meta, ((0, 0), (0, samples.shape[1] - capacity)))[:, None, :]
    arrived = lax.all_to_all(
        jnp.concatenate([send_samples, meta_row], axis=1), "tile", split_axis=0, concat_axis=0, tiled=True
    )
    slot_total = tile_count * capacity
    arrived_meta = arrived[:, capacity, :capacity].astype(jnp.int32).reshape(slot_total)
    arrived = arrived[:, :capacity, :].reshape(slot_total, samples.shape[1])

    slab_rows = G // tile_count
    row_cells = slab_rows // S
    cell_cols = G // S
    q_len = G // NF
    q_cells = q_len // S
    j_len = P_SIZE // NF

    cell_r = arrived_meta // NW
    plane_r = arrived_meta % NW
    p2 = patches_rotated(arrived, plane_r, kernel_set).reshape(slot_total * 2, S * 2 * S)

    a_s = cell_r // cell_cols
    cc_s = cell_r % cell_cols
    p_s = cc_s // q_cells
    qc_s = cc_s % q_cells
    resid = jnp.arange(NF, dtype=jnp.int32)
    a_c = jnp.repeat(a_s, 2)[None, :]
    qc_c = jnp.repeat(qc_s, 2)[None, :]
    p_c = jnp.repeat(p_s, 2)[None, :]
    k_c = (jnp.arange(slot_total * 2, dtype=jnp.int32) % 2)[None, :]
    ph_index = jnp.mod(spacing * (p_c - NF // 2) * resid[:, None], NF)
    half = math.sqrt(0.5)
    cos_v = jnp.where(
        ph_index == 0,
        1.0,
        jnp.where(
            ph_index == 4,
            -1.0,
            jnp.where((ph_index == 2) | (ph_index == 6), 0.0, jnp.where((ph_index == 1) | (ph_index == 7), half, -half)),
        ),
    )
    sin_v = jnp.where(
        (ph_index == 0) | (ph_index == 4),
        0.0,
        jnp.where(
            ph_index == 2,
            1.0,
            jnp.where(ph_index == 6, -1.0, jnp.where((ph_index == 1) | (ph_index == 3), half, -half)),
        ),
    )
    phase = jnp.where(k_c == 0, cos_v, sin_v)
    cell_id = jnp.arange(row_cells * q_cells, dtype=jnp.int32)[:, None]
    inside = (a_c == cell_id // q_cells) & (qc_c == cell_id % q_cells)
    l2 = jnp.where(inside[None, :, :], phase[:, None, :], 0.0).astype(jnp.bfloat16)
    l2 = l2.reshape(NF * row_cells * q_cells, slot_total * 2)
    folded = jnp.dot(l2, p2, preferred_element_type=jnp.float32).astype(jnp.bfloat16)
    folded = folded.reshape(NF, row_cells, q_cells, S, 2 * S)

    coarse = jnp.arange(q_cells, dtype=jnp.int32) * S
    fine = jnp.arange(S, dtype=jnp.int32)
    n_full = jnp.arange(2 * j_len, dtype=jnp.int32) % j_len
    j_full = resid[:, None] + NF * (n_full[None, :] - j_len // 2)
    y_full = jnp.arange(2 * S, dtype=jnp.int32) % S
    ca, sa = cos_sin_f32(jnp.mod(coarse[None, :, None] * (spacing * j_full[:, None, :]), G))
    cb, sb = cos_sin_f32(jnp.mod(y_full[None, :, None] * (spacing * j_full[:, None, :]), G))
    ca = ca[:, :, None, :]
    sa = sa[:, :, None, :]
    cb = cb[:, None, :, :]
    sb = sb[:, None, :, :]
    c1 = (ca * cb - sa * sb).astype(jnp.bfloat16)
    s1 = (sa * cb + ca * sb).astype(jnp.bfloat16)
    ri_in = lax.broadcasted_iota(jnp.int32, (1, 1, 2 * S, 2 * j_len), 2) // S
    ri_out = lax.broadcasted_iota(jnp.int32, (1, 1, 2 * S, 2 * j_len), 3) // j_len
    w1 = jnp.where(ri_in == ri_out, c1, jnp.where(ri_in == 0, s1, -s1))
    transformed = jnp.einsum("raqxk,rqkn->raxn", folded, w1, preferred_element_type=jnp.float32)
    transformed = transformed.astype(jnp.bfloat16).reshape(NF, slab_rows, 2, j_len)

    l_index = jnp.arange(P_SIZE, dtype=jnp.int32) - P_SIZE // 2
    row_base = (tile_index * slab_rows - G // 2) + jnp.arange(row_cells, dtype=jnp.int32) * S
    ca, sa = cos_sin_f32(phase_index(l_index, row_base))
    cb, sb = cos_sin_f32(phase_index(l_index, fine))
    c2 = (ca[:, :, None] * cb[:, None, :] - sa[:, :, None] * sb[:, None, :]).astype(jnp.bfloat16)
    s2 = (sa[:, :, None] * cb[:, None, :] + ca[:, :, None] * sb[:, None, :]).astype(jnp.bfloat16)
    c2 = c2.reshape(P_SIZE, slab_rows)
    s2 = s2.reshape(P_SIZE, slab_rows)
    e2 = jnp.stack([c2, -s2], axis=1)
    partial = jnp.einsum("liu,ruij->lrj", e2, transformed, preferred_element_type=jnp.float32)
    chan_count = lax.axis_size("chan")
    partial = partial.reshape(chan_count, P_SIZE // chan_count, NF, j_len)
    partial = lax.all_to_all(partial.astype(jnp.bfloat16), "chan", split_axis=0, concat_axis=0, tiled=True)
    partial = jnp.sum(partial.astype(jnp.float32), axis=0)
    partial = partial.reshape(P_SIZE // chan_count, NF, tile_count, j_len // tile_count)
    partial = jnp.transpose(partial, (2, 0, 1, 3))
    partial = lax.all_to_all(partial.astype(jnp.bfloat16), "tile", split_axis=0, concat_axis=0, tiled=True)
    partial = jnp.sum(partial.astype(jnp.float32), axis=0)
    out = jnp.transpose(partial, (0, 2, 1))
    return out.reshape(out.shape[0], -1) * (1.0 / G)


def solution(mesh):
    placed = (
        P("chan", "tile", None),
        P("chan", None, None, None, None),
        P("chan", "tile", None),
        P("chan", "tile"),
        P("chan", "tile"),
    )
    return jax.shard_map(
        local, mesh=mesh, in_specs=placed, out_specs=P("chan", "tile"), check_vma=False
    )
```

profile of v0, /device:TPU:0, one launch (start us, length us, event | category | flops | bytes accessed | tf_op | source)
XLA Modules:
  0.0 240.3 jit_solution(11238614292134303467)
XLA Ops:
  0.0 0.8 fusion.54
  1.6 0.7 iota_compare_fusion.3
  2.3 0.8 fusion.51
  3.1 0.7 convert_bitcast_fusion.1
  4.0 1.4 fusion.30
  5.8 0.8 pad_maximum_fusion.1
  6.6 7.3 %all-to-all-start = ((f32[8,97,128]{2,1,0:T(8,128)}), f32[8,97,128]{2,1,0:T(8,128)}, u32[]{:S(2)}, u32[]{:S(2)}) async-start(f32[8,97,128]{2,1,0:T(8,128)} %pad_maximum_fusion.1), calls=%async_computation | async-start | bytes 851968 | tf_op jit(solution)/shard_map/all_to_all | solution.py:122
  13.9 1.4 slice_bitcast_fusion.1
  15.3 1.0 fusion.74
  16.6 1.1 fusion.38
  18.0 2.0 subtract_convert_fusion.2
  20.7 2.0 copy.28
  22.7 3.1 %reshape.791.u_ref = bf16[32,64,128]{2,1,0:T(8,128)(2,1)} reshape(bf16[32,64,2,64]{3,2,1,0:T(2,128)(2,1)} %copy.28) | data formatting | bytes 1048576 | tf_op jit(solution)/shard_map/reshape | solution.py:63
  25.8 4.5 %convert_element_type.143 = bf16[4,256,1,1024]{1,0,3,2:T(4,128)(2,1)} reshape(bf16[1024,16,64]{0,2,1:T(8,128)(2,1)} %subtract_convert_fusion.2) | data formatting | bytes 4194304 | tf_op jit(solution)/shard_map/convert_element_type | solution.py:200
  30.3 4.3 %copy.21 = bf16[4,256,1,1024]{3,1,2,0:T(8,128)(2,1)} copy(bf16[4,256,1,1024]{1,0,3,2:T(4,128)(2,1)} %convert_element_type.143) | data formatting | bytes 4194304 | tf_op jit(solution)/shard_map/convert_element_type | solution.py:200
  34.7 2.8 %neg.21 = bf16[4,256,1,1024]{1,0,3,2:T(4,128)(2,1)} reshape(bf16[1024,16,64]{0,2,1:T(8,128)(2,1)S(1)} %fusion.19) | data formatting | bytes 4194304 | tf_op jit(solution)/shard_map/neg | solution.py:204
  37.4 4.4 %copy.22 = bf16[4,256,1,1024]{3,1,2,0:T(8,128)(2,1)} copy(bf16[4,256,1,1024]{1,0,3,2:T(4,128)(2,1)} %neg.21) | data formatting | bytes 4194304 | tf_op jit(solution)/shard_map/neg | solution.py:204
  42.4 1.1 pad_maximum_fusion.v_ref
  44.2 4.1 %fusion.26 = (f32[8,128,256]{2,1,0:T(8,128)S(1)}, f32[8,128,256]{2,1,0:T(8,128)S(1)}) fusion(s32[8,256]{1,0:T(8,128)S(1)} %add_multiply_fusion, s32[128]{0:T(128)S(1)} %and_select_fusion), kind=kLoop, calls=%fused_computation.45 | loop fusion | flops 3670016 | bytes 2105856 | tf_op jit(solution)/shard_map/cos | solution.py:96
  48.4 0.8 fusion.58
  49.9 1.0 slice.40
  50.9 0.9 copy.26
  53.5 3.5 %select_convert_fusion = bf16[8,256,1536]{2,1,0:T(8,128)(2,1)} fusion(bf16[8,1536]{1,0:T(8,128)(2,1)S(1)} %select_select_fusion, pred[256,1536]{1,0:T(8,128)(4,1)S(1)} %compare_and_fusion), kind=kLoop, calls=%fused_computation.6 | loop fusion | flops 3145728 | bytes 6709248 | tf_op jit(solution)/shard_map/convert_element_type | solution.py:172
  57.0 20.0 %shard_map.55 = bf16[768,2,64,128]{3,2,1,0:T(8,128)(2,1)} custom-call(s32[768]{0:T(1024)} %get-tuple-element.17.plane_ref, f32[128,768]{1,0:T(8,128)} %bitcast.96, bf16[32,64,128]{2,1,0:T(8,128)(2,1)} %reshape.791.u_ref, bf16[32,2,64,128]{3,2,1,0:T(8,128)(2,1)} %pad_maximum_fusion.v_ref), custom_call_target="tpu_custom_call" | custom-call | flops 3221225472 | bytes 50331648 | tf_op jit(solution)/shard_map/pallas_call | solution.py:79
  77.0 59.9 %convert_bitcast_fusion = bf16[256,8,64,128]{3,1,2,0:T(8,128)(2,1)} fusion(bf16[2048,1536]{1,0:T(8,128)(2,1)} %bitcast.92, bf16[192,8,64,128]{3,2,1,0:T(8,128)(2,1)} %bitcast.88), kind=kOutput, calls=%fused_computation | convolution fusion | flops 51556384768 | bytes 65011712 | tf_op jit(solution)/shard_map/dot_general | solution.py:174
  136.9 23.1 %copy.42 = bf16[256,8,64,128]{3,2,1,0:T(8,128)(2,1)} copy(bf16[256,8,64,128]{3,1,2,0:T(8,128)(2,1)} %convert_bitcast_fusion) | data formatting | bytes 67108864
  160.0 16.2 %bitcast_convert_fusion = bf16[8,16,64,256]{3,2,1,0:T(8,128)(2,1)} fusion(bf16[8,16,16,64,128]{4,3,2,1,0:T(8,128)(2,1)} %bitcast.87, f32[8,128,256]{2,1,0:T(8,128)S(1)} %get-tuple-element.12, f32[8,16,256]{2,1,0:T(8,128)S(1)} %get-tuple-element.10, f32[8,128,256]{2,1,0:T(8,128)S(1)} %get-tuple-element.11, f32[8,16,256]{2,1,0:T(8,128)S(1)} %get-tuple-element.9, ...), kind=kOutput, calls=%fused_computation.10 | convolution fusion | flops 8638169088 | bytes 40173568 | tf_op jit(solution)/shard_map/raqxk,rqkn->raxn/dot_general | solution.py:193
  176.1 7.1 %reshape.794 = bf16[8,1024,2,128]{3,2,1,0:T(2,128)(2,1)} reshape(bf16[8,16,64,256]{3,2,1,0:T(8,128)(2,1)} %bitcast_convert_fusion) | data formatting | bytes 8388608 | tf_op jit(solution)/shard_map/reshape | solution.py:194
  183.2 7.3 %bitcast_convert_fusion.1 = bf16[4,256,8,128]{3,1,2,0:T(8,128)(2,1)S(1)} fusion(bf16[8,1024,2,128]{3,2,1,0:T(2,128)(2,1)} %reshape.794, bf16[4,256,1,1024]{3,1,2,0:T(8,128)(2,1)} %copy.22, bf16[4,256,1,1024]{3,1,2,0:T(8,128)(2,1)S(1)} %copy-done.1), kind=kOutput, calls=%fused_computation.21 | convolution fusion | flops 4304404480 | bytes 10485760 | tf_op jit(solution)/shard_map/liu,ruij->lrj/dot_general | solution.py:205
  190.5 28.3 %all_to_all.15 = bf16[4,256,8,128]{3,1,2,0:T(8,128)(2,1)S(1)} all-to-all(bf16[4,256,8,128]{3,1,2,0:T(8,128)(2,1)S(1)} %bitcast_convert_fusion.1), channel_id=1, replica_groups=mesh['tile'=8,'chan'=4] {'chan'}, dimensions={0} | all-to-all | bytes 4194304 | tf_op jit(solution)/shard_map/all_to_all | solution.py:208
  219.5 19.9 %all_to_all.16 = bf16[8,256,8,16]{1,3,2,0:T(8,128)(2,1)S(1)} all-to-all(bf16[8,256,8,16]{1,3,2,0:T(8,128)(2,1)S(1)} %copy.32), channel_id=1, replica_groups=mesh['tile'=8,'chan'=4] {'tile'}, dimensions={0} | all-to-all | bytes 1048576 | tf_op jit(solution)/shard_map/all_to_all | solution.py:212
  239.6 0.8 copy.35
  (60 shorter events, 6.9 us)
Async XLA Ops:
  0.0 13.9 %copy-start.4 = (bf16[1,32,2,64,128]{4,3,2,1,0:T(8,128)(2,1)S(1)}, bf16[1,32,2,64,128]{4,3,2,1,0:T(8,128)(2,1)}, u32[]{:S(2)}) copy-start(bf16[1,32,2,64,128]{4,3,2,1,0:T(8,128)(2,1)} %param.6) | copy-start | bytes 3145732
  6.6 41.8 %all-to-all-start = ((f32[8,97,128]{2,1,0:T(8,128)}), f32[8,97,128]{2,1,0:T(8,128)}, u32[]{:S(2)}, u32[]{:S(2)}) async-start(f32[8,97,128]{2,1,0:T(8,128)} %pad_maximum_fusion.1), calls=%async_computation | async-start | bytes 851968 | tf_op jit(solution)/shard_map/all_to_all | solution.py:122
  34.7 7.2 %copy-start = (bf16[32,64,64]{2,1,0:T(8,128)(2,1)S(1)}, bf16[32,64,64]{2,1,0:T(8,128)(2,1)}, u32[]{:S(2)}) copy-start(bf16[32,64,64]{2,1,0:T(8,128)(2,1)} %fusion.74) | copy-start | bytes 786436
  34.7 7.2 %copy-start.2 = (bf16[32,64,64]{2,1,0:T(8,128)(2,1)S(1)}, bf16[32,64,64]{2,1,0:T(8,128)(2,1)}, u32[]{:S(2)}) copy-start(bf16[32,64,64]{2,1,0:T(8,128)(2,1)} %get-tuple-element.5) | copy-start | bytes 786436
  37.4 4.4 %copy-start.3 = (bf16[32,64,64]{2,1,0:T(8,128)(2,1)S(1)}, bf16[32,64,64]{2,1,0:T(8,128)(2,1)}, u32[]{:S(2)}) copy-start(bf16[32,64,64]{2,1,0:T(8,128)(2,1)} %get-tuple-element.6) | copy-start | bytes 786436
  176.1 7.1 %copy-start.1 = (bf16[4,256,1,1024]{3,1,2,0:T(8,128)(2,1)S(1)}, bf16[4,256,1,1024]{3,1,2,0:T(8,128)(2,1)}, u32[]{:S(2)}) copy-start(bf16[4,256,1,1024]{3,1,2,0:T(8,128)(2,1)} %copy.21) | copy-start | bytes 6291460
where the time goes:
time: 241 us; the launch traced here: 240 us
  matrix products  84.8 us (35%)
  local copies, waits for them, and re-layouts  57.7 us (24%)
  blocking collectives  48.2 us (20%)
  other arithmetic  22 us (9%)
  Pallas kernels  20 us (8%)
  starting transfers between devices  7.25 us (3%)
    dot_general x1, matrix products, local(): jnp.dot(l2, p2, preferred_element_type=jnp.float32).astype(jnp.bfloat16)  59.9 us
    all_to_all x1, blocking collectives, local(): lax.all_to_all(partial.astype(jnp.bfloat16), 'chan', split_axis=0, concat...  28.3 us
    unnamed x12, local copies, waits for them, and re-layouts  23.2 us
    pallas_call x1, Pallas kernels, patches_rotated(): pl.pallas_call(patch_kernel, grid_spec=grid_spec, out_shape=jax.ShapeDtyp...  20 us
    all_to_all x1, blocking collectives, local(): lax.all_to_all(partial.astype(jnp.bfloat16), 'tile', split_axis=0, concat...  19.9 us
    dot_general x1, matrix products, local(): jnp.einsum('raqxk,rqkn->raxn', folded, w1, preferred_element_type=jnp.flo...  16.2 us
    convert_element_type x2, local copies, waits for them, and re-layouts, local(): (ca[:, :, None] * cb[:, None, :] - sa[:, :, None] * sb[:, None, :]).astyp...  8.84 us
    dot_general x1, matrix products, local(): jnp.einsum('liu,ruij->lrj', e2, transformed, preferred_element_type=jnp.f...  7.31 us
  transfers between devices with their start and end apart: 1, of which 0 were waited for; matrix products, arithmetic and copies ran while one was open for 14% of the time, Pallas kernels for 0%

commit v1 on v0

--- a/solution.py
+++ b/solution.py
@@ -191,18 +191,20 @@
     ri_out = lax.broadcasted_iota(jnp.int32, (1, 1, 2 * S, 2 * j_len), 3) // j_len
     w1 = jnp.where(ri_in == ri_out, c1, jnp.where(ri_in == 0, s1, -s1))
     transformed = jnp.einsum("raqxk,rqkn->raxn", folded, w1, preferred_element_type=jnp.float32)
-    transformed = transformed.astype(jnp.bfloat16).reshape(NF, slab_rows, 2, j_len)
+    transformed = transformed.astype(jnp.bfloat16).reshape(NF, slab_rows, 2 * j_len)
 
     l_index = jnp.arange(P_SIZE, dtype=jnp.int32) - P_SIZE // 2
-    row_base = (tile_index * slab_rows - G // 2) + jnp.arange(row_cells, dtype=jnp.int32) * S
-    ca, sa = cos_sin_f32(phase_index(l_index, row_base))
-    cb, sb = cos_sin_f32(phase_index(l_index, fine))
+    lane_blocks = slab_rows // 128
+    block_base = (tile_index * slab_rows - G // 2) + jnp.arange(lane_blocks, dtype=jnp.int32) * 128
+    ca, sa = cos_sin_f32(phase_index(l_index, block_base))
+    cb, sb = cos_sin_f32(phase_index(l_index, jnp.arange(128, dtype=jnp.int32)))
     c2 = (ca[:, :, None] * cb[:, None, :] - sa[:, :, None] * sb[:, None, :]).astype(jnp.bfloat16)
     s2 = (sa[:, :, None] * cb[:, None, :] + ca[:, :, None] * sb[:, None, :]).astype(jnp.bfloat16)
     c2 = c2.reshape(P_SIZE, slab_rows)
     s2 = s2.reshape(P_SIZE, slab_rows)
-    e2 = jnp.stack([c2, -s2], axis=1)
-    partial = jnp.einsum("liu,ruij->lrj", e2, transformed, preferred_element_type=jnp.float32)
+    partial = jnp.einsum(
+        "lu,ruj->lrj", c2, transformed[:, :, :j_len], preferred_element_type=jnp.float32
+    ) - jnp.einsum("lu,ruj->lrj", s2, transformed[:, :, j_len:], preferred_element_type=jnp.float32)
     chan_count = lax.axis_size("chan")
     partial = partial.reshape(chan_count, P_SIZE // chan_count, NF, j_len)
     partial = lax.all_to_all(partial.astype(jnp.bfloat16), "chan", split_axis=0, concat_axis=0, tiled=True)

time: 241 us -> 228 us (0.946)
  local copies, waits for them, and re-layouts: 57.7 us -> 39.6 us
  other arithmetic: 22 us -> 30.1 us
  matrix products: 84.8 us -> 81 us
    neg x2 -> x0, local copies, waits for them, and re-layouts: 7.15 us -> none  [local(): e2 = jnp.stack([c2, -s2], axis=1)]
    reshape x1 -> x0, local copies, waits for them, and re-layouts: 7.08 us -> none  [local(): transformed.astype(jnp.bfloat16).reshape(NF, slab_rows, 2, j_len)]
    convert_element_type x2 -> x1, local copies, waits for them, and re-layouts: 8.84 us -> 2.32 us  [local(): (ca[:, :, None] * cb[:, None, :] - sa[:, :, None] * sb[:, None, :]).astyp...]
    convert_element_type x1, other arithmetic: 2.02 us -> 8.36 us  [local(): (ca[:, :, None] * cb[:, None, :] - sa[:, :, None] * sb[:, None, :]).astyp...]
    convert_element_type x0 -> x1, local copies, waits for them, and re-layouts: none -> 4.23 us  [local(): (sa[:, :, None] * cb[:, None, :] + ca[:, :, None] * sb[:, None, :]).astyp...]
    dot_general x1 -> x2, matrix products: 7.31 us -> 4.68 us  [the longest x1 2.34 us: local(): jnp.einsum('lu,ruj->lrj', c2, transformed[:, :, :j_len], preferred_elemen...]
    unnamed x12 -> x10, local copies, waits for them, and re-layouts: 23.2 us -> 23.2 us
where the time goes in v1:
time: 228 us; the launch traced here: 227 us
  matrix products  81 us (36%)
  blocking collectives  48.2 us (21%)
  local copies, waits for them, and re-layouts  39.6 us (17%)
  other arithmetic  30.1 us (13%)
  Pallas kernels  20.1 us (9%)
  starting transfers between devices  7.25 us (3%)
    dot_general x1, matrix products, local(): jnp.dot(l2, p2, preferred_element_type=jnp.float32).astype(jnp.bfloat16)  59.9 us
    all_to_all x1, blocking collectives, local(): lax.all_to_all(partial.astype(jnp.bfloat16), 'chan', split_axis=0, concat...  28.3 us
    unnamed x10, local copies, waits for them, and re-layouts  23.2 us
    pallas_call x1, Pallas kernels, patches_rotated(): pl.pallas_call(patch_kernel, grid_spec=grid_spec, out_shape=jax.ShapeDtyp...  20.1 us
    all_to_all x1, blocking collectives, local(): lax.all_to_all(partial.astype(jnp.bfloat16), 'tile', split_axis=0, concat...  19.9 us
    dot_general x1, matrix products, local(): jnp.einsum('raqxk,rqkn->raxn', folded, w1, preferred_element_type=jnp.flo...  14.9 us
    convert_element_type x1, other arithmetic, local(): (ca[:, :, None] * cb[:, None, :] - sa[:, :, None] * sb[:, None, :]).astyp...  8.36 us
    cos x4, other arithmetic, cos_sin_f32(): return (jnp.cos(angle), jnp.sin(angle))  8.14 us
  transfers between devices with their start and end apart: 1, of which 0 were waited for; matrix products, arithmetic and copies ran while one was open for 14% of the time, Pallas kernels for 0%

profile of v1, /device:TPU:0, one launch (start us, length us, event | category | flops | bytes accessed | tf_op | source)
XLA Modules:
  0.0 226.5 jit_solution(10397600132592157224)
XLA Ops:
  0.0 0.8 fusion.52
  1.6 0.7 iota_compare_fusion.3
  2.3 0.8 fusion.49
  3.1 0.7 convert_bitcast_fusion.1
  4.0 1.4 fusion.28
  5.8 0.8 pad_maximum_fusion.1
  6.6 7.3 %all-to-all-start = ((f32[8,97,128]{2,1,0:T(8,128)}), f32[8,97,128]{2,1,0:T(8,128)}, u32[]{:S(2)}, u32[]{:S(2)}) async-start(f32[8,97,128]{2,1,0:T(8,128)} %pad_maximum_fusion.1), calls=%async_computation | async-start | bytes 851968 | tf_op jit(solution)/shard_map/all_to_all | solution.py:122
  13.9 1.4 slice_bitcast_fusion.1
  15.8 0.8 copy.38
  16.6 1.3 reshape.698.u_ref
  17.9 3.2 %fusion.33 = (f32[1024,128]{1,0:T(8,128)}, f32[1024,128]{1,0:T(8,128)}) fusion(s32[128]{0:T(128)S(1)} %iota_multiply_fusion.1, s32[1024]{0:T(1024)S(1)} %iota_add_fusion), kind=kLoop, calls=%fused_computation.58 | loop fusion | flops 1835008 | bytes 1053184 | tf_op jit(solution)/shard_map/cos | solution.py:96
  21.5 1.0 copy.32
  22.5 8.4 %subtract_convert_fusion.3 = (bf16[1024,8,128]{2,1,0:T(8,128)(2,1)S(1)}, bf16[1024,8,128]{2,1,0:T(8,128)(2,1)}) fusion(f32[1024,128]{1,0:T(8,128)} %get-tuple-element.18, f32[1024,8]{1,0:T(8,128)} %copy.32, f32[1024,128]{1,0:T(8,128)} %get-tuple-element.17, f32[1024,8]{1,0:T(8,128)S(1)} %copy.31), kind=kLoop, calls=%fused_computation.19 | loop fusion | flops 8388608 | bytes 5308416 | tf_op jit(solution)/shard_map/convert_element_type | solution.py:201
  30.9 4.2 %reshape.705 = bf16[1024,1024,1]{1,0,2:T(8,128)(2,1)} reshape(bf16[1024,8,128]{2,1,0:T(8,128)(2,1)} %get-tuple-element.6) | data formatting | bytes 4194304 | tf_op jit(solution)/shard_map/convert_element_type | solution.py:202
  35.1 2.3 %reshape.704 = bf16[1024,1024,1]{1,0,2:T(8,128)(2,1)} reshape(bf16[1024,8,128]{2,1,0:T(8,128)(2,1)S(1)} %get-tuple-element.5) | data formatting | bytes 4194304 | tf_op jit(solution)/shard_map/convert_element_type | solution.py:201
  37.4 1.8 maximum_bitcast_fusion
  39.2 1.1 pad_maximum_fusion.v_ref
  41.1 4.1 %fusion.27 = (f32[8,128,256]{2,1,0:T(8,128)S(1)}, f32[8,128,256]{2,1,0:T(8,128)S(1)}) fusion(s32[8,256]{1,0:T(8,128)S(1)} %add_multiply_fusion, s32[128]{0:T(128)S(1)} %and_select_fusion), kind=kLoop, calls=%fused_computation.50 | loop fusion | flops 3670016 | bytes 2105856 | tf_op jit(solution)/shard_map/cos | solution.py:96
  45.2 0.8 fusion.56
  46.1 0.6 add_select_fusion.6
  46.7 1.0 slice.48
  47.7 0.9 copy.36
  50.3 3.5 %select_convert_fusion = bf16[8,256,1536]{2,1,0:T(8,128)(2,1)} fusion(bf16[8,1536]{1,0:T(8,128)(2,1)S(1)} %select_select_fusion, pred[256,1536]{1,0:T(8,128)(4,1)S(1)} %compare_and_fusion), kind=kLoop, calls=%fused_computation.6 | loop fusion | flops 3145728 | bytes 6709248 | tf_op jit(solution)/shard_map/convert_element_type | solution.py:172
  53.8 20.1 %shard_map.55 = bf16[768,2,64,128]{3,2,1,0:T(8,128)(2,1)} custom-call(s32[768]{0:T(1024)} %get-tuple-element.19.plane_ref, f32[128,768]{1,0:T(8,128)} %bitcast.80, bf16[32,64,128]{2,1,0:T(8,128)(2,1)} %reshape.698.u_ref, bf16[32,2,64,128]{3,2,1,0:T(8,128)(2,1)} %pad_maximum_fusion.v_ref), custom_call_target="tpu_custom_call" | custom-call | flops 3221225472 | bytes 50331648 | tf_op jit(solution)/shard_map/pallas_call | solution.py:79
  73.9 59.9 %convert_bitcast_fusion = bf16[256,8,64,128]{3,1,2,0:T(8,128)(2,1)} fusion(bf16[2048,1536]{1,0:T(8,128)(2,1)} %bitcast.75, bf16[192,8,64,128]{3,2,1,0:T(8,128)(2,1)} %bitcast.71), kind=kOutput, calls=%fused_computation | convolution fusion | flops 51556384768 | bytes 65011712 | tf_op jit(solution)/shard_map/dot_general | solution.py:174
  133.8 23.1 %copy.52 = bf16[256,8,64,128]{3,2,1,0:T(8,128)(2,1)} copy(bf16[256,8,64,128]{3,1,2,0:T(8,128)(2,1)} %convert_bitcast_fusion) | data formatting | bytes 67108864
  156.9 14.9 %bitcast_convert_fusion = bf16[8,16,64,256]{3,2,1,0:T(8,128)(2,1)S(1)} fusion(bf16[8,16,16,64,128]{4,3,2,1,0:T(8,128)(2,1)} %bitcast.70, f32[8,128,256]{2,1,0:T(8,128)S(1)} %get-tuple-element.14, f32[8,16,256]{2,1,0:T(8,128)S(1)} %get-tuple-element.12, f32[8,128,256]{2,1,0:T(8,128)S(1)} %get-tuple-element.13, f32[8,16,256]{2,1,0:T(8,128)S(1)} %get-tuple-element.11, ...), kind=kOutput, calls=%fused_computation.10 | convolution fusion | flops 8638169088 | bytes 40173568 | tf_op jit(solution)/shard_map/raqxk,rqkn->raxn/dot_general | solution.py:193
  171.9 2.3 %fusion.14 = f32[1024,8,128]{2,0,1:T(8,128)S(1)} fusion(bf16[1024,1024,1]{1,0,2:T(8,128)(2,1)S(1)} %copy-done, bf16[8,1024,256]{2,1,0:T(8,128)(2,1)S(1)} %bitcast.88), kind=kOutput, calls=%fused_computation.20 | convolution fusion | flops 2147483648 | bytes 8388608 | tf_op jit(solution)/shard_map/lu,ruj->lrj/dot_general | solution.py:207
  174.3 2.3 %subtract_convert_fusion.2 = bf16[1024,8,128]{2,0,1:T(8,128)(2,1)S(1)} fusion(f32[1024,8,128]{2,0,1:T(8,128)S(1)} %fusion.14, bf16[1024,1024,1]{1,0,2:T(8,128)(2,1)S(1)} %copy-done.1, bf16[8,1024,256]{2,1,0:T(8,128)(2,1)S(1)} %bitcast.89), kind=kOutput, calls=%fused_computation.17 | convolution fusion | flops 2149580800 | bytes 10485760 | tf_op jit(solution)/shard_map/lu,ruj->lrj/dot_general | solution.py:205
  176.8 28.3 %all_to_all.15 = bf16[4,256,8,128]{3,1,2,0:T(8,128)(2,1)S(1)} all-to-all(bf16[4,256,8,128]{3,1,2,0:T(8,128)(2,1)S(1)} %copy.40), channel_id=1, replica_groups=mesh['tile'=8,'chan'=4] {'chan'}, dimensions={0} | all-to-all | bytes 4194304 | tf_op jit(solution)/shard_map/all_to_all | solution.py:210
  205.7 19.9 %all_to_all.16 = bf16[8,256,8,16]{1,3,2,0:T(8,128)(2,1)S(1)} all-to-all(bf16[8,256,8,16]{1,3,2,0:T(8,128)(2,1)S(1)} %copy.43), channel_id=1, replica_groups=mesh['tile'=8,'chan'=4] {'tile'}, dimensions={0} | all-to-all | bytes 1048576 | tf_op jit(solution)/shard_map/all_to_all | solution.py:214
  225.8 0.8 copy.46
  (58 shorter events, 5.5 us)
Async XLA Ops:
  0.0 13.8 %copy-start.3 = (bf16[1,32,2,64,128]{4,3,2,1,0:T(8,128)(2,1)S(1)}, bf16[1,32,2,64,128]{4,3,2,1,0:T(8,128)(2,1)}, u32[]{:S(2)}) copy-start(bf16[1,32,2,64,128]{4,3,2,1,0:T(8,128)(2,1)} %param.6) | copy-start | bytes 3145732
  6.6 38.6 %all-to-all-start = ((f32[8,97,128]{2,1,0:T(8,128)}), f32[8,97,128]{2,1,0:T(8,128)}, u32[]{:S(2)}, u32[]{:S(2)}) async-start(f32[8,97,128]{2,1,0:T(8,128)} %pad_maximum_fusion.1), calls=%async_computation | async-start | bytes 851968 | tf_op jit(solution)/shard_map/all_to_all | solution.py:122
  30.9 6.5 %copy-start.2 = (bf16[32,64,64]{2,1,0:T(8,128)(2,1)S(1)}, bf16[32,64,64]{2,1,0:T(8,128)(2,1)}, u32[]{:S(2)}) copy-start(bf16[32,64,64]{2,1,0:T(8,128)(2,1)} %get-tuple-element.7) | copy-start | bytes 786436
  156.9 14.9 %copy-start = (bf16[1024,1024,1]{1,0,2:T(8,128)(2,1)S(1)}, bf16[1024,1024,1]{1,0,2:T(8,128)(2,1)}, u32[]{:S(2)}) copy-start(bf16[1024,1024,1]{1,0,2:T(8,128)(2,1)} %reshape.705) | copy-start | bytes 6291460
  171.9 2.4 %copy-start.1 = (bf16[1024,1024,1]{1,0,2:T(8,128)(2,1)S(1)}, bf16[1024,1024,1]{1,0,2:T(8,128)(2,1)}, u32[]{:S(2)}) copy-start(bf16[1024,1024,1]{1,0,2:T(8,128)(2,1)} %reshape.704) | copy-start | bytes 6291460

commit v2 on v1

--- a/solution.py
+++ b/solution.py
@@ -206,12 +206,13 @@
         "lu,ruj->lrj", c2, transformed[:, :, :j_len], preferred_element_type=jnp.float32
     ) - jnp.einsum("lu,ruj->lrj", s2, transformed[:, :, j_len:], preferred_element_type=jnp.float32)
     chan_count = lax.axis_size("chan")
-    partial = partial.reshape(chan_count, P_SIZE // chan_count, NF, j_len)
-    partial = lax.all_to_all(partial.astype(jnp.bfloat16), "chan", split_axis=0, concat_axis=0, tiled=True)
-    partial = jnp.sum(partial.astype(jnp.float32), axis=0)
-    partial = partial.reshape(P_SIZE // chan_count, NF, tile_count, j_len // tile_count)
-    partial = jnp.transpose(partial, (2, 0, 1, 3))
-    partial = lax.all_to_all(partial.astype(jnp.bfloat16), "tile", split_axis=0, concat_axis=0, tiled=True)
+    partial = partial.reshape(chan_count, P_SIZE // chan_count, NF, tile_count, j_len // tile_count)
+    partial = jnp.transpose(partial, (0, 3, 1, 2, 4)).reshape(
+        chan_count * tile_count, P_SIZE // chan_count, NF, j_len // tile_count
+    )
+    partial = lax.all_to_all(
+        partial.astype(jnp.bfloat16), ("chan", "tile"), split_axis=0, concat_axis=0, tiled=True
+    )
     partial = jnp.sum(partial.astype(jnp.float32), axis=0)
     out = jnp.transpose(partial, (0, 2, 1))
     return out.reshape(out.shape[0], -1) * (1.0 / G)

time: 228 us -> 244 us (1.070)
  blocking collectives: 48.2 us -> 55.9 us
  local copies, waits for them, and re-layouts: 39.6 us -> 46.8 us
    all_to_all x2 -> x1, blocking collectives: 48.2 us -> 55.9 us  [local(): lax.all_to_all(partial.astype(jnp.bfloat16), ('chan', 'tile'), split_axis...]
    convert_element_type x2 -> x3, local copies, waits for them, and re-layouts: 0.18 us -> 7.6 us  [local(): partial.astype(jnp.bfloat16)]
  transfers between devices with their start and end apart: 1 -> 1, of which waited for: 0 -> 0; matrix products, arithmetic and copies ran while one was open for 14% -> 13% of each run, Pallas kernels for 0% -> 0%
where the time goes in v2:
time: 244 us; the launch traced here: 243 us
  matrix products  82.3 us (34%)
  blocking collectives  55.9 us (23%)
  local copies, waits for them, and re-layouts  46.8 us (19%)
  other arithmetic  29.9 us (12%)
  Pallas kernels  20.1 us (8%)
  starting transfers between devices  7.25 us (3%)
    dot_general x1, matrix products, local(): jnp.dot(l2, p2, preferred_element_type=jnp.float32).astype(jnp.bfloat16)  59.9 us
    all_to_all x1, blocking collectives, local(): lax.all_to_all(partial.astype(jnp.bfloat16), ('chan', 'tile'), split_axis...  55.9 us
    unnamed x10, local copies, waits for them, and re-layouts  23.2 us
    pallas_call x1, Pallas kernels, patches_rotated(): pl.pallas_call(patch_kernel, grid_spec=grid_spec, out_shape=jax.ShapeDtyp...  20.1 us
    dot_general x1, matrix products, local(): jnp.einsum('raqxk,rqkn->raxn', folded, w1, preferred_element_type=jnp.flo...  14.9 us
    convert_element_type x1, other arithmetic, local(): (ca[:, :, None] * cb[:, None, :] - sa[:, :, None] * sb[:, None, :]).astyp...  8.36 us
    cos x4, other arithmetic, cos_sin_f32(): return (jnp.cos(angle), jnp.sin(angle))  8.14 us
    convert_element_type x3, local copies, waits for them, and re-layouts, local(): partial.astype(jnp.bfloat16)  7.6 us
  transfers between devices with their start and end apart: 1, of which 0 were waited for; matrix products, arithmetic and copies ran while one was open for 13% of the time, Pallas kernels for 0%

profile of v2, /device:TPU:0, one launch (start us, length us, event | category | flops | bytes accessed | tf_op | source)
XLA Modules:
  0.0 242.6 jit_solution(10818795928956879933)
XLA Ops:
  0.0 0.8 fusion.52
  2.3 0.8 fusion.49
  3.1 0.7 convert_bitcast_fusion.1
  4.0 1.4 fusion.28
  5.8 0.8 pad_maximum_fusion.1
  6.6 7.3 %all-to-all-start = ((f32[8,97,128]{2,1,0:T(8,128)}), f32[8,97,128]{2,1,0:T(8,128)}, u32[]{:S(2)}, u32[]{:S(2)}) async-start(f32[8,97,128]{2,1,0:T(8,128)} %pad_maximum_fusion.1), calls=%async_computation | async-start | bytes 851968 | tf_op jit(solution)/shard_map/all_to_all | solution.py:122
  13.9 1.4 slice_bitcast_fusion.1
  15.8 0.8 copy.37
  16.6 1.3 reshape.698.u_ref
  17.9 3.2 %fusion.33 = (f32[1024,128]{1,0:T(8,128)}, f32[1024,128]{1,0:T(8,128)}) fusion(s32[128]{0:T(128)S(1)} %iota_multiply_fusion.1, s32[1024]{0:T(1024)S(1)} %iota_add_fusion), kind=kLoop, calls=%fused_computation.58 | loop fusion | flops 1835008 | bytes 1053184 | tf_op jit(solution)/shard_map/cos | solution.py:96
  21.5 1.0 copy.31
  22.5 8.4 %subtract_convert_fusion.3 = (bf16[1024,8,128]{2,1,0:T(8,128)(2,1)S(1)}, bf16[1024,8,128]{2,1,0:T(8,128)(2,1)}) fusion(f32[1024,128]{1,0:T(8,128)} %get-tuple-element.18, f32[1024,8]{1,0:T(8,128)} %copy.31, f32[1024,128]{1,0:T(8,128)} %get-tuple-element.17, f32[1024,8]{1,0:T(8,128)S(1)} %copy.30), kind=kLoop, calls=%fused_computation.20 | loop fusion | flops 8388608 | bytes 5308416 | tf_op jit(solution)/shard_map/convert_element_type | solution.py:201
  30.9 4.2 %reshape.705 = bf16[1024,1024,1]{1,0,2:T(8,128)(2,1)} reshape(bf16[1024,8,128]{2,1,0:T(8,128)(2,1)} %get-tuple-element.6) | data formatting | bytes 4194304 | tf_op jit(solution)/shard_map/convert_element_type | solution.py:202
  35.1 2.3 reshape.704
  37.4 1.8 maximum_bitcast_fusion
  39.2 1.1 pad_maximum_fusion.v_ref
  41.1 4.1 %fusion.27 = (f32[8,128,256]{2,1,0:T(8,128)S(1)}, f32[8,128,256]{2,1,0:T(8,128)S(1)}) fusion(s32[8,256]{1,0:T(8,128)S(1)} %add_multiply_fusion, s32[128]{0:T(128)S(1)} %and_select_fusion), kind=kLoop, calls=%fused_computation.50 | loop fusion | flops 3670016 | bytes 2105856 | tf_op jit(solution)/shard_map/cos | solution.py:96
  45.2 0.8 fusion.56
  46.7 1.0 slice.48
  47.7 0.9 copy.35
  50.3 3.5 %select_convert_fusion = bf16[8,256,1536]{2,1,0:T(8,128)(2,1)} fusion(bf16[8,1536]{1,0:T(8,128)(2,1)S(1)} %select_select_fusion, pred[256,1536]{1,0:T(8,128)(4,1)S(1)} %compare_and_fusion), kind=kLoop, calls=%fused_computation.6 | loop fusion | flops 3145728 | bytes 6709248 | tf_op jit(solution)/shard_map/convert_element_type | solution.py:172
  53.8 20.1 %shard_map.55 = bf16[768,2,64,128]{3,2,1,0:T(8,128)(2,1)} custom-call(s32[768]{0:T(1024)} %get-tuple-element.19.plane_ref, f32[128,768]{1,0:T(8,128)} %bitcast.80, bf16[32,64,128]{2,1,0:T(8,128)(2,1)} %reshape.698.u_ref, bf16[32,2,64,128]{3,2,1,0:T(8,128)(2,1)} %pad_maximum_fusion.v_ref), custom_call_target="tpu_custom_call" | custom-call | flops 3221225472 | bytes 50331648 | tf_op jit(solution)/shard_map/pallas_call | solution.py:79
  73.9 59.9 %convert_bitcast_fusion = bf16[256,8,64,128]{3,1,2,0:T(8,128)(2,1)} fusion(bf16[2048,1536]{1,0:T(8,128)(2,1)} %bitcast.77, bf16[192,8,64,128]{3,2,1,0:T(8,128)(2,1)} %bitcast.71), kind=kOutput, calls=%fused_computation | convolution fusion | flops 51556384768 | bytes 65011712 | tf_op jit(solution)/shard_map/dot_general | solution.py:174
  133.8 23.1 %copy.46 = bf16[256,8,64,128]{3,2,1,0:T(8,128)(2,1)} copy(bf16[256,8,64,128]{3,1,2,0:T(8,128)(2,1)} %convert_bitcast_fusion) | data formatting | bytes 67108864
  156.9 14.9 %bitcast_convert_fusion = bf16[8,16,64,256]{3,2,1,0:T(8,128)(2,1)S(1)} fusion(bf16[8,16,16,64,128]{4,3,2,1,0:T(8,128)(2,1)} %bitcast.70, f32[8,128,256]{2,1,0:T(8,128)S(1)} %get-tuple-element.14, f32[8,16,256]{2,1,0:T(8,128)S(1)} %get-tuple-element.12, f32[8,128,256]{2,1,0:T(8,128)S(1)} %get-tuple-element.13, f32[8,16,256]{2,1,0:T(8,128)S(1)} %get-tuple-element.11, ...), kind=kOutput, calls=%fused_computation.10 | convolution fusion | flops 8638169088 | bytes 40173568 | tf_op jit(solution)/shard_map/raqxk,rqkn->raxn/dot_general | solution.py:193
  171.9 2.3 fusion.14
  174.3 3.7 %subtract_convert_fusion.2 = bf16[1024,8,128]{2,0,1:T(8,128)(2,1)} fusion(f32[1024,8,128]{2,0,1:T(8,128)S(1)} %fusion.14, bf16[1024,1024,1]{1,0,2:T(8,128)(2,1)S(1)} %copy-done.1, bf16[8,1024,256]{2,1,0:T(8,128)(2,1)S(1)} %bitcast.89), kind=kOutput, calls=%fused_computation.18 | convolution fusion | flops 2149580800 | bytes 10485760 | tf_op jit(solution)/shard_map/lu,ruj->lrj/dot_general | solution.py:205
  178.0 2.9 %copy.39 = bf16[1024,8,128]{0,2,1:T(8,128)(2,1)S(1)} copy(bf16[1024,8,128]{2,0,1:T(8,128)(2,1)} %subtract_convert_fusion.2) | data formatting | bytes 4194304 | tf_op jit(solution)/shard_map/convert_element_type | solution.py:214
  180.8 2.8 %convert_element_type.148 = bf16[4,256,8,8,16]{1,0,4,3,2:T(4,128)(2,1)} reshape(bf16[1024,8,128]{0,2,1:T(8,128)(2,1)S(1)} %copy.39) | data formatting | bytes 4194304 | tf_op jit(solution)/shard_map/convert_element_type | solution.py:214
  183.6 2.0 copy.40
  185.6 55.9 %all_to_all.10 = bf16[32,256,8,16]{1,3,2,0:T(8,128)(2,1)S(1)} all-to-all(bf16[32,256,8,16]{1,3,2,0:T(8,128)(2,1)S(1)} %bitcast.76), channel_id=1, replica_groups=mesh['tile'=8,'chan'=4] {'chan','tile'}, dimensions={0} | all-to-all | bytes 4194304 | tf_op jit(solution)/shard_map/all_to_all | solution.py:213
  241.9 0.8 copy.42
  (56 shorter events, 6.3 us)
Async XLA Ops:
  0.0 13.8 %copy-start.3 = (bf16[1,32,2,64,128]{4,3,2,1,0:T(8,128)(2,1)S(1)}, bf16[1,32,2,64,128]{4,3,2,1,0:T(8,128)(2,1)}, u32[]{:S(2)}) copy-start(bf16[1,32,2,64,128]{4,3,2,1,0:T(8,128)(2,1)} %param.6) | copy-start | bytes 3145732
  6.6 38.6 %all-to-all-start = ((f32[8,97,128]{2,1,0:T(8,128)}), f32[8,97,128]{2,1,0:T(8,128)}, u32[]{:S(2)}, u32[]{:S(2)}) async-start(f32[8,97,128]{2,1,0:T(8,128)} %pad_maximum_fusion.1), calls=%async_computation | async-start | bytes 851968 | tf_op jit(solution)/shard_map/all_to_all | solution.py:122
  30.9 6.5 %copy-start.2 = (bf16[32,64,64]{2,1,0:T(8,128)(2,1)S(1)}, bf16[32,64,64]{2,1,0:T(8,128)(2,1)}, u32[]{:S(2)}) copy-start(bf16[32,64,64]{2,1,0:T(8,128)(2,1)} %get-tuple-element.7) | copy-start | bytes 786436
  156.9 14.9 %copy-start = (bf16[1024,1024,1]{1,0,2:T(8,128)(2,1)S(1)}, bf16[1024,1024,1]{1,0,2:T(8,128)(2,1)}, u32[]{:S(2)}) copy-start(bf16[1024,1024,1]{1,0,2:T(8,128)(2,1)} %reshape.705) | copy-start | bytes 6291460
  171.9 2.4 copy-start.1

commit v3 on v1

--- a/solution.py
+++ b/solution.py
@@ -172,7 +172,7 @@
     l2 = jnp.where(inside[None, :, :], phase[:, None, :], 0.0).astype(jnp.bfloat16)
     l2 = l2.reshape(NF * row_cells * q_cells, slot_total * 2)
     folded = jnp.dot(l2, p2, preferred_element_type=jnp.float32).astype(jnp.bfloat16)
-    folded = folded.reshape(NF, row_cells, q_cells, S, 2 * S)
+    folded = folded.reshape(NF, row_cells, q_cells // 8, 8, S, 2 * S)
 
     coarse = jnp.arange(q_cells, dtype=jnp.int32) * S
     fine = jnp.arange(S, dtype=jnp.int32)
@@ -190,7 +190,7 @@
     ri_in = lax.broadcasted_iota(jnp.int32, (1, 1, 2 * S, 2 * j_len), 2) // S
     ri_out = lax.broadcasted_iota(jnp.int32, (1, 1, 2 * S, 2 * j_len), 3) // j_len
     w1 = jnp.where(ri_in == ri_out, c1, jnp.where(ri_in == 0, s1, -s1))
-    transformed = jnp.einsum("raqxk,rqkn->raxn", folded, w1, preferred_element_type=jnp.float32)
+    transformed = jnp.einsum("rahqxk,rhqkn->raxn", folded, w1.reshape(NF, q_cells // 8, 8, 2 * S, 2 * j_len), preferred_element_type=jnp.float32)
     transformed = transformed.astype(jnp.bfloat16).reshape(NF, slab_rows, 2 * j_len)
 
     l_index = jnp.arange(P_SIZE, dtype=jnp.int32) - P_SIZE // 2

time: 228 us -> 211 us (0.925)
  local copies, waits for them, and re-layouts: 39.6 us -> 16.4 us
  matrix products: 81 us -> 87.8 us
    unnamed x10 -> x9, local copies, waits for them, and re-layouts: 23.2 us -> 0.09 us
    dot_general x1, matrix products: 14.9 us -> 21.8 us  [local(): jnp.einsum('rahqxk,rhqkn->raxn', folded, w1.reshape(NF, q_cells // 8, 8,...]
  transfers between devices with their start and end apart: 1 -> 1, of which waited for: 0 -> 0; matrix products, arithmetic and copies ran while one was open for 14% -> 15% of each run, Pallas kernels for 0% -> 0%
where the time goes in v3:
time: 211 us; the launch traced here: 210 us
  matrix products  87.8 us (42%)
  blocking collectives  48.2 us (23%)
  other arithmetic  30.1 us (14%)
  Pallas kernels  20.1 us (10%)
  local copies, waits for them, and re-layouts  16.4 us (8%)
  starting transfers between devices  7.25 us (3%)
    dot_general x1, matrix products, local(): jnp.dot(l2, p2, preferred_element_type=jnp.float32).astype(jnp.bfloat16)  59.9 us
    all_to_all x1, blocking collectives, local(): lax.all_to_all(partial.astype(jnp.bfloat16), 'chan', split_axis=0, concat...  28.3 us
    dot_general x1, matrix products, local(): jnp.einsum('rahqxk,rhqkn->raxn', folded, w1.reshape(NF, q_cells // 8, 8,...  21.8 us
    pallas_call x1, Pallas kernels, patches_rotated(): pl.pallas_call(patch_kernel, grid_spec=grid_spec, out_shape=jax.ShapeDtyp...  20.1 us
    all_to_all x1, blocking collectives, local(): lax.all_to_all(partial.astype(jnp.bfloat16), 'tile', split_axis=0, concat...  19.9 us
    convert_element_type x1, other arithmetic, local(): (ca[:, :, None] * cb[:, None, :] - sa[:, :, None] * sb[:, None, :]).astyp...  8.36 us
    cos x4, other arithmetic, cos_sin_f32(): return (jnp.cos(angle), jnp.sin(angle))  8.14 us
    all_to_all x1, starting transfers between devices, local(): lax.all_to_all(jnp.concatenate([send_samples, meta_row], axis=1), 'tile',...  7.25 us
  transfers between devices with their start and end apart: 1, of which 0 were waited for; matrix products, arithmetic and copies ran while one was open for 15% of the time, Pallas kernels for 0%

profile of v3, /device:TPU:0, one launch (start us, length us, event | category | flops | bytes accessed | tf_op | source)
XLA Modules:
  0.0 210.2 jit_solution(10579626809328104573)
XLA Ops:
  0.0 0.8 fusion.55
  1.6 0.7 iota_compare_fusion.3
  2.3 0.8 fusion.52
  3.1 0.7 convert_bitcast_fusion
  4.0 1.4 fusion.31
  5.8 0.8 pad_maximum_fusion.1
  6.6 7.3 %all-to-all-start = ((f32[8,97,128]{2,1,0:T(8,128)}), f32[8,97,128]{2,1,0:T(8,128)}, u32[]{:S(2)}, u32[]{:S(2)}) async-start(f32[8,97,128]{2,1,0:T(8,128)} %pad_maximum_fusion.1), calls=%async_computation | async-start | bytes 851968 | tf_op jit(solution)/shard_map/all_to_all | solution.py:122
  13.9 1.4 slice_bitcast_fusion.1
  15.8 0.8 copy.41
  16.6 1.3 reshape.710.u_ref
  17.9 3.2 %fusion.36 = (f32[1024,128]{1,0:T(8,128)}, f32[1024,128]{1,0:T(8,128)}) fusion(s32[128]{0:T(128)S(1)} %iota_multiply_fusion, s32[1024]{0:T(1024)S(1)} %iota_add_fusion), kind=kLoop, calls=%fused_computation.59 | loop fusion | flops 1835008 | bytes 1053184 | tf_op jit(solution)/shard_map/cos | solution.py:96
  21.5 1.0 copy.35
  22.5 8.4 %subtract_convert_fusion.3 = (bf16[1024,8,128]{2,1,0:T(8,128)(2,1)S(1)}, bf16[1024,8,128]{2,1,0:T(8,128)(2,1)}) fusion(f32[1024,128]{1,0:T(8,128)} %get-tuple-element.18, f32[1024,8]{1,0:T(8,128)} %copy.35, f32[1024,128]{1,0:T(8,128)} %get-tuple-element.17, f32[1024,8]{1,0:T(8,128)S(1)} %copy.34), kind=kLoop, calls=%fused_computation.20 | loop fusion | flops 8388608 | bytes 5308416 | tf_op jit(solution)/shard_map/convert_element_type | solution.py:201
  30.9 4.2 %reshape.717 = bf16[1024,1024,1]{1,0,2:T(8,128)(2,1)} reshape(bf16[1024,8,128]{2,1,0:T(8,128)(2,1)} %get-tuple-element.6) | data formatting | bytes 4194304 | tf_op jit(solution)/shard_map/convert_element_type | solution.py:202
  35.1 2.3 %reshape.716 = bf16[1024,1024,1]{1,0,2:T(8,128)(2,1)} reshape(bf16[1024,8,128]{2,1,0:T(8,128)(2,1)S(1)} %get-tuple-element.5) | data formatting | bytes 4194304 | tf_op jit(solution)/shard_map/convert_element_type | solution.py:201
  37.5 1.8 maximum_bitcast_fusion
  39.2 1.1 pad_maximum_fusion.v_ref
  40.5 0.6 fusion.41
  41.1 4.1 %fusion.30 = (f32[8,128,256]{2,1,0:T(8,128)S(1)}, f32[8,128,256]{2,1,0:T(8,128)S(1)}) fusion(s32[8,256]{1,0:T(8,128)S(1)} %add_multiply_fusion, s32[128]{0:T(128)S(1)} %and_select_fusion), kind=kLoop, calls=%fused_computation.51 | loop fusion | flops 3670016 | bytes 2105856 | tf_op jit(solution)/shard_map/cos | solution.py:96
  45.2 0.8 fusion.59
  46.1 0.6 add_select_fusion.6
  46.7 1.0 slice.48
  47.7 0.9 copy.39
  50.3 3.5 %select_convert_fusion = bf16[8,256,1536]{2,1,0:T(8,128)(2,1)} fusion(bf16[8,1536]{1,0:T(8,128)(2,1)S(1)} %select_select_fusion, pred[256,1536]{1,0:T(8,128)(4,1)S(1)} %compare_and_fusion), kind=kLoop, calls=%fused_computation.8 | loop fusion | flops 3145728 | bytes 6709248 | tf_op jit(solution)/shard_map/convert_element_type | solution.py:172
  53.8 20.1 %shard_map.55 = bf16[768,2,64,128]{3,2,1,0:T(8,128)(2,1)} custom-call(s32[768]{0:T(1024)} %get-tuple-element.19.plane_ref, f32[128,768]{1,0:T(8,128)} %bitcast.76, bf16[32,64,128]{2,1,0:T(8,128)(2,1)} %reshape.710.u_ref, bf16[32,2,64,128]{3,2,1,0:T(8,128)(2,1)} %pad_maximum_fusion.v_ref), custom_call_target="tpu_custom_call" | custom-call | flops 3221225472 | bytes 50331648 | tf_op jit(solution)/shard_map/pallas_call | solution.py:79
  73.9 59.9 %convolution_convert_fusion = bf16[2048,8192]{1,0:T(8,128)(2,1)} fusion(bf16[2048,1536]{1,0:T(8,128)(2,1)} %bitcast.71, bf16[192,8,64,128]{3,2,1,0:T(8,128)(2,1)} %bitcast.67), kind=kOutput, calls=%fused_computation.2 | convolution fusion | flops 51556384768 | bytes 65011712 | tf_op jit(solution)/shard_map/dot_general | solution.py:174
  133.8 21.8 %bitcast_convert_fusion = bf16[8,16,64,256]{3,2,1,0:T(8,128)(2,1)S(1)} fusion(f32[8,128,256]{2,1,0:T(8,128)S(1)} %get-tuple-element.14, f32[8,2,8,256]{3,2,1,0:T(8,128)S(1)} %get-tuple-element.12, f32[8,128,256]{2,1,0:T(8,128)S(1)} %get-tuple-element.13, f32[8,2,8,256]{3,2,1,0:T(8,128)S(1)} %get-tuple-element.11, ...), kind=kOutput, calls=%fused_computation.11 | convolution fusion | flops 8638169088 | bytes 40173568 | tf_op jit(solution)/shard_map/rahqxk,rhqkn->raxn/dot_general | solution.py:193
  155.6 2.3 %fusion.17 = f32[1024,8,128]{2,0,1:T(8,128)S(1)} fusion(bf16[1024,1024,1]{1,0,2:T(8,128)(2,1)S(1)} %copy-done, bf16[8,1024,256]{2,1,0:T(8,128)(2,1)S(1)} %bitcast.85), kind=kOutput, calls=%fused_computation.21 | convolution fusion | flops 2147483648 | bytes 8388608 | tf_op jit(solution)/shard_map/lu,ruj->lrj/dot_general | solution.py:207
  157.9 2.3 %subtract_convert_fusion.2 = bf16[1024,8,128]{2,0,1:T(8,128)(2,1)S(1)} fusion(f32[1024,8,128]{2,0,1:T(8,128)S(1)} %fusion.17, bf16[1024,1024,1]{1,0,2:T(8,128)(2,1)S(1)} %copy-done.1, bf16[8,1024,256]{2,1,0:T(8,128)(2,1)S(1)} %bitcast.86), kind=kOutput, calls=%fused_computation.18 | convolution fusion | flops 2149580800 | bytes 10485760 | tf_op jit(solution)/shard_map/lu,ruj->lrj/dot_general | solution.py:205
  160.4 28.3 %all_to_all.15 = bf16[4,256,8,128]{3,1,2,0:T(8,128)(2,1)S(1)} all-to-all(bf16[4,256,8,128]{3,1,2,0:T(8,128)(2,1)S(1)} %copy.44), channel_id=1, replica_groups=mesh['tile'=8,'chan'=4] {'chan'}, dimensions={0} | all-to-all | bytes 4194304 | tf_op jit(solution)/shard_map/all_to_all | solution.py:210
  189.4 19.9 %all_to_all.16 = bf16[8,256,8,16]{1,3,2,0:T(8,128)(2,1)S(1)} all-to-all(bf16[8,256,8,16]{1,3,2,0:T(8,128)(2,1)S(1)} %copy.47), channel_id=1, replica_groups=mesh['tile'=8,'chan'=4] {'tile'}, dimensions={0} | all-to-all | bytes 1048576 | tf_op jit(solution)/shard_map/all_to_all | solution.py:214
  209.5 0.8 copy.50
  (57 shorter events, 4.9 us)
Async XLA Ops:
  0.0 13.9 %copy-start.3 = (bf16[1,32,2,64,128]{4,3,2,1,0:T(8,128)(2,1)S(1)}, bf16[1,32,2,64,128]{4,3,2,1,0:T(8,128)(2,1)}, u32[]{:S(2)}) copy-start(bf16[1,32,2,64,128]{4,3,2,1,0:T(8,128)(2,1)} %param.6) | copy-start | bytes 3145732
  6.6 38.6 %all-to-all-start = ((f32[8,97,128]{2,1,0:T(8,128)}), f32[8,97,128]{2,1,0:T(8,128)}, u32[]{:S(2)}, u32[]{:S(2)}) async-start(f32[8,97,128]{2,1,0:T(8,128)} %pad_maximum_fusion.1), calls=%async_computation | async-start | bytes 851968 | tf_op jit(solution)/shard_map/all_to_all | solution.py:122
  30.9 6.6 %copy-start.2 = (bf16[32,64,64]{2,1,0:T(8,128)(2,1)S(1)}, bf16[32,64,64]{2,1,0:T(8,128)(2,1)}, u32[]{:S(2)}) copy-start(bf16[32,64,64]{2,1,0:T(8,128)(2,1)} %get-tuple-element.7) | copy-start | bytes 786436
  133.8 21.8 %copy-start = (bf16[1024,1024,1]{1,0,2:T(8,128)(2,1)S(1)}, bf16[1024,1024,1]{1,0,2:T(8,128)(2,1)}, u32[]{:S(2)}) copy-start(bf16[1024,1024,1]{1,0,2:T(8,128)(2,1)} %reshape.717) | copy-start | bytes 6291460
  155.6 2.3 %copy-start.1 = (bf16[1024,1024,1]{1,0,2:T(8,128)(2,1)S(1)}, bf16[1024,1024,1]{1,0,2:T(8,128)(2,1)}, u32[]{:S(2)}) copy-start(bf16[1024,1024,1]{1,0,2:T(8,128)(2,1)} %reshape.716) | copy-start | bytes 6291460

commit v4 on v3

--- a/solution.py
+++ b/solution.py
@@ -181,6 +181,7 @@
     y_full = jnp.arange(2 * S, dtype=jnp.int32) % S
     ca, sa = cos_sin_f32(jnp.mod(coarse[None, :, None] * (spacing * j_full[:, None, :]), G))
     cb, sb = cos_sin_f32(jnp.mod(y_full[None, :, None] * (spacing * j_full[:, None, :]), G))
+    ca, sa, cb, sb = lax.optimization_barrier((ca, sa, cb, sb))
     ca = ca[:, :, None, :]
     sa = sa[:, :, None, :]
     cb = cb[:, None, :, :]
@@ -198,6 +199,7 @@
     block_base = (tile_index * slab_rows - G // 2) + jnp.arange(lane_blocks, dtype=jnp.int32) * 128
     ca, sa = cos_sin_f32(phase_index(l_index, block_base))
     cb, sb = cos_sin_f32(phase_index(l_index, jnp.arange(128, dtype=jnp.int32)))
+    ca, sa, cb, sb = lax.optimization_barrier((ca, sa, cb, sb))
     c2 = (ca[:, :, None] * cb[:, None, :] - sa[:, :, None] * sb[:, None, :]).astype(jnp.bfloat16)
     s2 = (sa[:, :, None] * cb[:, None, :] + ca[:, :, None] * sb[:, None, :]).astype(jnp.bfloat16)
     c2 = c2.reshape(P_SIZE, slab_rows)

time: 211 us -> 210 us (level)
    sin x0 -> x4, other arithmetic: none -> 10.7 us  [cos_sin_f32(): return (jnp.cos(angle), jnp.sin(angle))]
    cos x4 -> x0, other arithmetic: 8.14 us -> none  [cos_sin_f32(): return (jnp.cos(angle), jnp.sin(angle))]
    convert_element_type x1, other arithmetic: 8.36 us -> 6.04 us  [local(): (ca[:, :, None] * cb[:, None, :] - sa[:, :, None] * sb[:, None, :]).astyp...]
  transfers between devices with their start and end apart: 1 -> 1, of which waited for: 0 -> 0; matrix products, arithmetic and copies ran while one was open for 15% -> 14% of each run, Pallas kernels for 0% -> 0%
where the time goes in v4:
time: 210 us
  matrix products  88.2 us (42%)
  blocking collectives  48.2 us (23%)
  other arithmetic  30.5 us (15%)
  Pallas kernels  20.1 us (10%)
  local copies, waits for them, and re-layouts  15.2 us (7%)
  starting transfers between devices  7.25 us (3%)
    dot_general x1, matrix products, local(): jnp.dot(l2, p2, preferred_element_type=jnp.float32).astype(jnp.bfloat16)  60 us
    all_to_all x1, blocking collectives, local(): lax.all_to_all(partial.astype(jnp.bfloat16), 'chan', split_axis=0, concat...  28.3 us
    dot_general x1, matrix products, local(): jnp.einsum('rahqxk,rhqkn->raxn', folded, w1.reshape(NF, q_cells // 8, 8,...  22 us
    pallas_call x1, Pallas kernels, patches_rotated(): pl.pallas_call(patch_kernel, grid_spec=grid_spec, out_shape=jax.ShapeDtyp...  20.1 us
    all_to_all x1, blocking collectives, local(): lax.all_to_all(partial.astype(jnp.bfloat16), 'tile', split_axis=0, concat...  19.9 us
    sin x4, other arithmetic, cos_sin_f32(): return (jnp.cos(angle), jnp.sin(angle))  10.7 us
    all_to_all x1, starting transfers between devices, local(): lax.all_to_all(jnp.concatenate([send_samples, meta_row], axis=1), 'tile',...  7.25 us
    convert_element_type x1, other arithmetic, local(): (ca[:, :, None] * cb[:, None, :] - sa[:, :, None] * sb[:, None, :]).astyp...  6.04 us
  transfers between devices with their start and end apart: 1, of which 0 were waited for; matrix products, arithmetic and copies ran while one was open for 14% of the time, Pallas kernels for 0%

profile of v4, /device:TPU:0, one launch (start us, length us, event | category | flops | bytes accessed | tf_op | source)
XLA Modules:
  0.0 209.8 jit_solution(4354636853568783910)
XLA Ops:
  0.0 0.8 fusion.55
  1.6 0.7 iota_compare_fusion.3
  2.3 0.8 fusion.52
  3.1 0.7 convert_bitcast_fusion
  4.0 1.4 fusion.34
  5.8 0.8 pad_maximum_fusion.1
  6.6 7.3 %all-to-all-start = ((f32[8,97,128]{2,1,0:T(8,128)}), f32[8,97,128]{2,1,0:T(8,128)}, u32[]{:S(2)}, u32[]{:S(2)}) async-start(f32[8,97,128]{2,1,0:T(8,128)} %pad_maximum_fusion.1), calls=%async_computation | async-start | bytes 851968 | tf_op jit(solution)/shard_map/all_to_all | solution.py:122
  13.9 1.4 slice_bitcast_fusion.1
  15.5 0.8 copy.24
  16.3 1.3 reshape.553.u_ref
  17.6 5.9 %fusion.32 = (f32[8,128,256]{2,1,0:T(8,128)}, f32[8,128,256]{2,1,0:T(8,128)}) fusion(s32[8,256]{1,0:T(8,128)S(1)} %add_multiply_fusion, s32[128]{0:T(128)S(1)} %and_select_fusion), kind=kLoop, calls=%fused_computation.58 | loop fusion | flops 3670016 | bytes 2105856 | tf_op jit(solution)/shard_map/sin | solution.py:96
  23.6 0.6 fusion.45
  24.2 2.1 %fusion.40 = (f32[1024,8]{1,0:T(8,128)S(1)}, f32[1024,8]{1,0:T(8,128)S(1)}) fusion(s32[8]{0:T(128)S(1)} %add_multiply_fusion.1, s32[1024]{0:T(1024)S(1)} %iota_add_fusion), kind=kLoop, calls=%fused_computation.68 | loop fusion | flops 114688 | bytes 69664 | tf_op jit(solution)/shard_map/sin | solution.py:96
  26.3 2.1 %fusion.38 = (f32[1024,128]{1,0:T(8,128)S(1)}, f32[1024,128]{1,0:T(8,128)S(1)}) fusion(s32[128]{0:T(128)S(1)} %iota_multiply_fusion.1, s32[1024]{0:T(1024)S(1)} %iota_add_fusion), kind=kLoop, calls=%fused_computation.66 | loop fusion | flops 1835008 | bytes 1053184 | tf_op jit(solution)/shard_map/sin | solution.py:96
  28.4 6.0 %subtract_convert_fusion.3 = (bf16[1024,8,128]{2,1,0:T(8,128)(2,1)S(1)}, bf16[1024,8,128]{2,1,0:T(8,128)(2,1)}) fusion(f32[1024,128]{1,0:T(8,128)S(1)} %get-tuple-element.16, f32[1024,8]{1,0:T(8,128)S(1)} %get-tuple-element.15, f32[1024,128]{1,0:T(8,128)S(1)} %get-tuple-element.14, f32[1024,8]{1,0:T(8,128)S(1)} %get-tuple-element.13), kind=kLoop, calls=%fused_computation.20 | loop fusion | flops 8388608 | bytes 5308416 | tf_op jit(solution)/shard_map/convert_element_type | solution.py:203
  34.5 4.2 %reshape.560 = bf16[1024,1024,1]{1,0,2:T(8,128)(2,1)} reshape(bf16[1024,8,128]{2,1,0:T(8,128)(2,1)} %get-tuple-element.22) | data formatting | bytes 4194304 | tf_op jit(solution)/shard_map/convert_element_type | solution.py:204
  38.6 2.3 %reshape.559 = bf16[1024,1024,1]{1,0,2:T(8,128)(2,1)} reshape(bf16[1024,8,128]{2,1,0:T(8,128)(2,1)S(1)} %get-tuple-element.21) | data formatting | bytes 4194304 | tf_op jit(solution)/shard_map/convert_element_type | solution.py:203
  41.2 1.9 maximum_bitcast_fusion
  43.1 1.1 pad_maximum_fusion.v_ref
  44.3 0.8 fusion.59
  45.2 0.6 add_select_fusion.6
  45.8 1.0 slice.48
  46.8 0.9 copy.22
  49.4 3.5 %select_convert_fusion = bf16[8,256,1536]{2,1,0:T(8,128)(2,1)} fusion(bf16[8,1536]{1,0:T(8,128)(2,1)S(1)} %select_select_fusion, pred[256,1536]{1,0:T(8,128)(4,1)S(1)} %compare_and_fusion), kind=kLoop, calls=%fused_computation.8 | loop fusion | flops 3145728 | bytes 6709248 | tf_op jit(solution)/shard_map/convert_element_type | solution.py:172
  52.9 20.1 %shard_map.55 = bf16[768,2,64,128]{3,2,1,0:T(8,128)(2,1)} custom-call(s32[768]{0:T(1024)} %get-tuple-element.35.plane_ref, f32[128,768]{1,0:T(8,128)} %bitcast.78, bf16[32,64,128]{2,1,0:T(8,128)(2,1)} %reshape.553.u_ref, bf16[32,2,64,128]{3,2,1,0:T(8,128)(2,1)} %pad_maximum_fusion.v_ref), custom_call_target="tpu_custom_call" | custom-call | flops 3221225472 | bytes 50331648 | tf_op jit(solution)/shard_map/pallas_call | solution.py:79
  73.1 60.0 %convolution_convert_fusion = bf16[2048,8192]{1,0:T(8,128)(2,1)} fusion(bf16[2048,1536]{1,0:T(8,128)(2,1)} %bitcast.73, bf16[192,8,64,128]{3,2,1,0:T(8,128)(2,1)} %bitcast.69), kind=kOutput, calls=%fused_computation.2 | convolution fusion | flops 51556384768 | bytes 65011712 | tf_op jit(solution)/shard_map/dot_general | solution.py:174
  133.1 22.0 %bitcast_convert_fusion = bf16[8,16,64,256]{3,2,1,0:T(8,128)(2,1)S(1)} fusion(f32[8,128,256]{2,1,0:T(8,128)S(1)} %copy-done.2, f32[8,2,8,256]{3,2,1,0:T(8,128)S(1)} %bitcast.81, f32[8,128,256]{2,1,0:T(8,128)S(1)} %copy-done.3, f32[8,2,8,256]{3,2,1,0:T(8,128)S(1)} %bitcast.82, pred[128,256]{1,0:T(8,128)(4,1)S(1)} %get-tuple-element.40, ...), kind=kOutput, calls=%fused_computation.11 | convolution fusion | flops 8638169088 | bytes 40173568 | tf_op jit(solution)/shard_map/rahqxk,rhqkn->raxn/dot_general | solution.py:194
  155.1 2.3 %fusion.17 = f32[1024,8,128]{2,0,1:T(8,128)S(1)} fusion(bf16[1024,1024,1]{1,0,2:T(8,128)(2,1)S(1)} %copy-done, bf16[8,1024,256]{2,1,0:T(8,128)(2,1)S(1)} %bitcast.89), kind=kOutput, calls=%fused_computation.21 | convolution fusion | flops 2147483648 | bytes 8388608 | tf_op jit(solution)/shard_map/lu,ruj->lrj/dot_general | solution.py:209
  157.5 2.3 %subtract_convert_fusion.2 = bf16[1024,8,128]{2,0,1:T(8,128)(2,1)S(1)} fusion(f32[1024,8,128]{2,0,1:T(8,128)S(1)} %fusion.17, bf16[1024,1024,1]{1,0,2:T(8,128)(2,1)S(1)} %copy-done.1, bf16[8,1024,256]{2,1,0:T(8,128)(2,1)S(1)} %bitcast.90), kind=kOutput, calls=%fused_computation.18 | convolution fusion | flops 2149580800 | bytes 10485760 | tf_op jit(solution)/shard_map/lu,ruj->lrj/dot_general | solution.py:207
  160.0 28.3 %all_to_all.15 = bf16[4,256,8,128]{3,1,2,0:T(8,128)(2,1)S(1)} all-to-all(bf16[4,256,8,128]{3,1,2,0:T(8,128)(2,1)S(1)} %copy.27), channel_id=1, replica_groups=mesh['tile'=8,'chan'=4] {'chan'}, dimensions={0} | all-to-all | bytes 4194304 | tf_op jit(solution)/shard_map/all_to_all | solution.py:212
  188.9 19.9 %all_to_all.16 = bf16[8,256,8,16]{1,3,2,0:T(8,128)(2,1)S(1)} all-to-all(bf16[8,256,8,16]{1,3,2,0:T(8,128)(2,1)S(1)} %copy.30), channel_id=1, replica_groups=mesh['tile'=8,'chan'=4] {'tile'}, dimensions={0} | all-to-all | bytes 1048576 | tf_op jit(solution)/shard_map/all_to_all | solution.py:216
  209.0 0.8 copy.33
  (57 shorter events, 4.5 us)
Async XLA Ops:
  0.0 13.8 %copy-start.4 = (bf16[1,32,2,64,128]{4,3,2,1,0:T(8,128)(2,1)S(1)}, bf16[1,32,2,64,128]{4,3,2,1,0:T(8,128)(2,1)}, u32[]{:S(2)}) copy-start(bf16[1,32,2,64,128]{4,3,2,1,0:T(8,128)(2,1)} %param.6) | copy-start | bytes 3145732
  6.6 37.7 %all-to-all-start = ((f32[8,97,128]{2,1,0:T(8,128)}), f32[8,97,128]{2,1,0:T(8,128)}, u32[]{:S(2)}, u32[]{:S(2)}) async-start(f32[8,97,128]{2,1,0:T(8,128)} %pad_maximum_fusion.1), calls=%async_computation | async-start | bytes 851968 | tf_op jit(solution)/shard_map/all_to_all | solution.py:122
  73.1 60.0 %copy-start.2 = (f32[8,128,256]{2,1,0:T(8,128)S(1)}, f32[8,128,256]{2,1,0:T(8,128)}, u32[]{:S(2)}) copy-start(f32[8,128,256]{2,1,0:T(8,128)} %get-tuple-element.20) | copy-start | bytes 3145732
  73.1 60.0 %copy-start.3 = (f32[8,128,256]{2,1,0:T(8,128)S(1)}, f32[8,128,256]{2,1,0:T(8,128)}, u32[]{:S(2)}) copy-start(f32[8,128,256]{2,1,0:T(8,128)} %get-tuple-element.18) | copy-start | bytes 3145732
  133.1 22.0 %copy-start = (bf16[1024,1024,1]{1,0,2:T(8,128)(2,1)S(1)}, bf16[1024,1024,1]{1,0,2:T(8,128)(2,1)}, u32[]{:S(2)}) copy-start(bf16[1024,1024,1]{1,0,2:T(8,128)(2,1)} %reshape.560) | copy-start | bytes 6291460
  155.1 2.3 %copy-start.1 = (bf16[1024,1024,1]{1,0,2:T(8,128)(2,1)S(1)}, bf16[1024,1024,1]{1,0,2:T(8,128)(2,1)}, u32[]{:S(2)}) copy-start(bf16[1024,1024,1]{1,0,2:T(8,128)(2,1)} %reshape.559) | copy-start | bytes 6291460

commit v5 on v4

--- a/solution.py
+++ b/solution.py
@@ -53,14 +53,14 @@
         rhs = jnp.concatenate(
             [jnp.concatenate([top, bottom], axis=1), jnp.concatenate([bottom, -top], axis=1)], axis=0
         )
-        both = jnp.dot(u_ref[w], rhs, preferred_element_type=jnp.float32)
-        out_ref[j, 0] = both[:, : 2 * S].astype(jnp.bfloat16)
-        out_ref[j, 1] = both[:, 2 * S :].astype(jnp.bfloat16)
+        both = lax.dot_general(u_ref[w], rhs, (((0,), (0,)), ((), ())), preferred_element_type=jnp.float32)
+        out_ref[j, 0] = both[:S, : 2 * S].astype(jnp.bfloat16)
+        out_ref[j, 1] = both[:S, 2 * S :].astype(jnp.bfloat16)
 
 
 def patches_rotated(samples, planes, kernel_set):
     slots = samples.shape[0]
-    u_kernel = jnp.transpose(kernel_set[:, :, :, :S], (0, 3, 1, 2)).reshape(NW, S, 2 * S)
+    u_kernel = kernel_set.reshape(NW, 2 * S, 2 * S)
     v_real = kernel_set[:, 0, :, S:]
     v_imag = kernel_set[:, 1, :, S:]
     v_parts = jnp.stack(
@@ -71,7 +71,7 @@
         grid=(slots // PATCH_CHUNK,),
         in_specs=[
             pl.BlockSpec((2 * S, PATCH_CHUNK), lambda i, p: (0, i)),
-            pl.BlockSpec((NW, S, 2 * S), lambda i, p: (0, 0, 0)),
+            pl.BlockSpec((NW, 2 * S, 2 * S), lambda i, p: (0, 0, 0)),
             pl.BlockSpec((NW, 2, S, 2 * S), lambda i, p: (0, 0, 0, 0)),
         ],
         out_specs=pl.BlockSpec((PATCH_CHUNK, 2, S, 2 * S), lambda i, p: (i, 0, 0, 0)),

time: 210 us -> 217 us (1.033)
  Pallas kernels: 20.1 us -> 28.9 us
  local copies, waits for them, and re-layouts: 15.2 us -> 13 us
    pallas_call x1, Pallas kernels: 20.1 us -> 28.9 us  [patches_rotated(): pl.pallas_call(patch_kernel, grid_spec=grid_spec, out_shape=jax.ShapeDtyp...]
  transfers between devices with their start and end apart: 1 -> 1, of which waited for: 0 -> 0; matrix products, arithmetic and copies ran while one was open for 14% -> 13% of each run, Pallas kernels for 0% -> 0%
where the time goes in v5:
time: 217 us; the launch traced here: 216 us
  matrix products  88.2 us (41%)
  blocking collectives  48.2 us (22%)
  other arithmetic  30.5 us (14%)
  Pallas kernels  28.9 us (13%)
  local copies, waits for them, and re-layouts  13 us (6%)
  starting transfers between devices  7.25 us (3%)
    dot_general x1, matrix products, local(): jnp.dot(l2, p2, preferred_element_type=jnp.float32).astype(jnp.bfloat16)  60 us
    pallas_call x1, Pallas kernels, patches_rotated(): pl.pallas_call(patch_kernel, grid_spec=grid_spec, out_shape=jax.ShapeDtyp...  28.9 us
    all_to_all x1, blocking collectives, local(): lax.all_to_all(partial.astype(jnp.bfloat16), 'chan', split_axis=0, concat...  28.3 us
    dot_general x1, matrix products, local(): jnp.einsum('rahqxk,rhqkn->raxn', folded, w1.reshape(NF, q_cells // 8, 8,...  22 us
    all_to_all x1, blocking collectives, local(): lax.all_to_all(partial.astype(jnp.bfloat16), 'tile', split_axis=0, concat...  19.9 us
    sin x4, other arithmetic, cos_sin_f32(): return (jnp.cos(angle), jnp.sin(angle))  10.8 us
    all_to_all x1, starting transfers between devices, local(): lax.all_to_all(jnp.concatenate([send_samples, meta_row], axis=1), 'tile',...  7.25 us
    convert_element_type x1, other arithmetic, local(): (ca[:, :, None] * cb[:, None, :] - sa[:, :, None] * sb[:, None, :]).astyp...  6.04 us
  transfers between devices with their start and end apart: 1, of which 0 were waited for; matrix products, arithmetic and copies ran while one was open for 13% of the time, Pallas kernels for 0%

profile of v5, /device:TPU:0, one launch (start us, length us, event | category | flops | bytes accessed | tf_op | source)
XLA Modules:
  0.0 216.4 jit_solution(17274548081172242800)
XLA Ops:
  0.0 0.8 fusion.55
  0.8 0.6 reduce-window.6
  1.6 0.7 iota_compare_fusion.3
  2.3 0.8 fusion.52
  3.1 0.7 convert_bitcast_fusion
  4.0 1.4 fusion.34
  5.8 0.8 pad_maximum_fusion.1
  6.6 7.3 %all-to-all-start = ((f32[8,97,128]{2,1,0:T(8,128)}), f32[8,97,128]{2,1,0:T(8,128)}, u32[]{:S(2)}, u32[]{:S(2)}) async-start(f32[8,97,128]{2,1,0:T(8,128)} %pad_maximum_fusion.1), calls=%async_computation | async-start | bytes 851968 | tf_op jit(solution)/shard_map/all_to_all | solution.py:122
  14.1 1.4 slice_bitcast_fusion
  15.5 6.0 %fusion.32 = (f32[8,128,256]{2,1,0:T(8,128)}, f32[8,128,256]{2,1,0:T(8,128)}) fusion(s32[8,256]{1,0:T(8,128)S(1)} %add_multiply_fusion, s32[128]{0:T(128)S(1)} %and_select_fusion), kind=kLoop, calls=%fused_computation.57 | loop fusion | flops 3670016 | bytes 2105856 | tf_op jit(solution)/shard_map/sin | solution.py:96
  21.4 0.6 fusion.45
  22.0 2.1 fusion.40
  24.1 2.1 fusion.38
  26.2 6.0 %subtract_convert_fusion.3 = (bf16[1024,8,128]{2,1,0:T(8,128)(2,1)S(1)}, bf16[1024,8,128]{2,1,0:T(8,128)(2,1)}) fusion(f32[1024,128]{1,0:T(8,128)S(1)} %get-tuple-element.16, f32[1024,8]{1,0:T(8,128)S(1)} %get-tuple-element.15, f32[1024,128]{1,0:T(8,128)S(1)} %get-tuple-element.14, f32[1024,8]{1,0:T(8,128)S(1)} %get-tuple-element.13), kind=kLoop, calls=%fused_computation.20 | loop fusion | flops 8388608 | bytes 5308416 | tf_op jit(solution)/shard_map/convert_element_type | solution.py:203
  32.3 4.2 %reshape.556 = bf16[1024,1024,1]{1,0,2:T(8,128)(2,1)} reshape(bf16[1024,8,128]{2,1,0:T(8,128)(2,1)} %get-tuple-element.22) | data formatting | bytes 4194304 | tf_op jit(solution)/shard_map/convert_element_type | solution.py:204
  36.5 2.3 %reshape.555 = bf16[1024,1024,1]{1,0,2:T(8,128)(2,1)} reshape(bf16[1024,8,128]{2,1,0:T(8,128)(2,1)S(1)} %get-tuple-element.21) | data formatting | bytes 4194304 | tf_op jit(solution)/shard_map/convert_element_type | solution.py:203
  39.0 1.9 maximum_bitcast_fusion
  41.0 1.1 pad_maximum_fusion.v_ref
  42.2 0.8 fusion.59
  43.0 0.6 add_select_fusion.6
  44.8 1.0 slice.44
  45.8 0.9 copy.21
  46.8 0.4 compare_and_fusion
  47.2 3.5 %select_convert_fusion = bf16[8,256,1536]{2,1,0:T(8,128)(2,1)} fusion(bf16[8,1536]{1,0:T(8,128)(2,1)S(1)} %select_select_fusion, pred[256,1536]{1,0:T(8,128)(4,1)S(1)} %compare_and_fusion), kind=kLoop, calls=%fused_computation.8 | loop fusion | flops 3145728 | bytes 6709248 | tf_op jit(solution)/shard_map/convert_element_type | solution.py:172
  50.7 28.9 %shard_map.55 = bf16[768,2,64,128]{3,2,1,0:T(8,128)(2,1)} custom-call(s32[768]{0:T(1024)} %get-tuple-element.35.plane_ref, f32[128,768]{1,0:T(8,128)} %bitcast.77, bf16[32,128,128]{2,1,0:T(8,128)(2,1)} %bitcast.72, bf16[32,2,64,128]{3,2,1,0:T(8,128)(2,1)} %pad_maximum_fusion.v_ref), custom_call_target="tpu_custom_call" | custom-call | flops 3221225472 | bytes 50331648 | tf_op jit(solution)/shard_map/pallas_call | solution.py:79
  79.6 60.0 %convolution_convert_fusion = bf16[2048,8192]{1,0:T(8,128)(2,1)} fusion(bf16[2048,1536]{1,0:T(8,128)(2,1)} %bitcast.71, bf16[192,8,64,128]{3,2,1,0:T(8,128)(2,1)} %bitcast.68), kind=kOutput, calls=%fused_computation.2 | convolution fusion | flops 51556384768 | bytes 65011712 | tf_op jit(solution)/shard_map/dot_general | solution.py:174
  139.7 22.0 %bitcast_convert_fusion = bf16[8,16,64,256]{3,2,1,0:T(8,128)(2,1)S(1)} fusion(f32[8,128,256]{2,1,0:T(8,128)S(1)} %copy-done.3, f32[8,2,8,256]{3,2,1,0:T(8,128)S(1)} %bitcast.80, f32[8,128,256]{2,1,0:T(8,128)S(1)} %copy-done.4, f32[8,2,8,256]{3,2,1,0:T(8,128)S(1)} %bitcast.81, pred[128,256]{1,0:T(8,128)(4,1)S(1)} %get-tuple-element.40, ...), kind=kOutput, calls=%fused_computation.11 | convolution fusion | flops 8638169088 | bytes 40173568 | tf_op jit(solution)/shard_map/rahqxk,rhqkn->raxn/dot_general | solution.py:194
  161.7 2.3 %fusion.17 = f32[1024,8,128]{2,0,1:T(8,128)S(1)} fusion(bf16[1024,1024,1]{1,0,2:T(8,128)(2,1)S(1)} %copy-done.1, bf16[8,1024,256]{2,1,0:T(8,128)(2,1)S(1)} %bitcast.88), kind=kOutput, calls=%fused_computation.21 | convolution fusion | flops 2147483648 | bytes 8388608 | tf_op jit(solution)/shard_map/lu,ruj->lrj/dot_general | solution.py:209
  164.1 2.3 %subtract_convert_fusion.2 = bf16[1024,8,128]{2,0,1:T(8,128)(2,1)S(1)} fusion(f32[1024,8,128]{2,0,1:T(8,128)S(1)} %fusion.17, bf16[1024,1024,1]{1,0,2:T(8,128)(2,1)S(1)} %copy-done.2, bf16[8,1024,256]{2,1,0:T(8,128)(2,1)S(1)} %bitcast.89), kind=kOutput, calls=%fused_computation.18 | convolution fusion | flops 2149580800 | bytes 10485760 | tf_op jit(solution)/shard_map/lu,ruj->lrj/dot_general | solution.py:207
  166.6 28.3 %all_to_all.15 = bf16[4,256,8,128]{3,1,2,0:T(8,128)(2,1)S(1)} all-to-all(bf16[4,256,8,128]{3,1,2,0:T(8,128)(2,1)S(1)} %copy.25), channel_id=1, replica_groups=mesh['tile'=8,'chan'=4] {'chan'}, dimensions={0} | all-to-all | bytes 4194304 | tf_op jit(solution)/shard_map/all_to_all | solution.py:212
  195.5 19.9 %all_to_all.16 = bf16[8,256,8,16]{1,3,2,0:T(8,128)(2,1)S(1)} all-to-all(bf16[8,256,8,16]{1,3,2,0:T(8,128)(2,1)S(1)} %copy.28), channel_id=1, replica_groups=mesh['tile'=8,'chan'=4] {'tile'}, dimensions={0} | all-to-all | bytes 1048576 | tf_op jit(solution)/shard_map/all_to_all | solution.py:216
  215.6 0.8 copy.31
  (54 shorter events, 3.5 us)
Async XLA Ops:
  0.0 14.0 %copy-start = (bf16[1,32,2,64,128]{4,3,2,1,0:T(8,128)(2,1)S(1)}, bf16[1,32,2,64,128]{4,3,2,1,0:T(8,128)(2,1)}, u32[]{:S(2)}) copy-start(bf16[1,32,2,64,128]{4,3,2,1,0:T(8,128)(2,1)} %param.6) | copy-start | bytes 3145732
  6.6 35.6 %all-to-all-start = ((f32[8,97,128]{2,1,0:T(8,128)}), f32[8,97,128]{2,1,0:T(8,128)}, u32[]{:S(2)}, u32[]{:S(2)}) async-start(f32[8,97,128]{2,1,0:T(8,128)} %pad_maximum_fusion.1), calls=%async_computation | async-start | bytes 851968 | tf_op jit(solution)/shard_map/all_to_all | solution.py:122
  79.6 60.0 %copy-start.3 = (f32[8,128,256]{2,1,0:T(8,128)S(1)}, f32[8,128,256]{2,1,0:T(8,128)}, u32[]{:S(2)}) copy-start(f32[8,128,256]{2,1,0:T(8,128)} %get-tuple-element.20) | copy-start | bytes 3145732
  79.6 60.0 %copy-start.4 = (f32[8,128,256]{2,1,0:T(8,128)S(1)}, f32[8,128,256]{2,1,0:T(8,128)}, u32[]{:S(2)}) copy-start(f32[8,128,256]{2,1,0:T(8,128)} %get-tuple-element.18) | copy-start | bytes 3145732
  139.7 22.0 %copy-start.1 = (bf16[1024,1024,1]{1,0,2:T(8,128)(2,1)S(1)}, bf16[1024,1024,1]{1,0,2:T(8,128)(2,1)}, u32[]{:S(2)}) copy-start(bf16[1024,1024,1]{1,0,2:T(8,128)(2,1)} %reshape.556) | copy-start | bytes 6291460
  161.7 2.3 %copy-start.2 = (bf16[1024,1024,1]{1,0,2:T(8,128)(2,1)S(1)}, bf16[1024,1024,1]{1,0,2:T(8,128)(2,1)}, u32[]{:S(2)}) copy-start(bf16[1024,1024,1]{1,0,2:T(8,128)(2,1)} %reshape.555) | copy-start | bytes 6291460
